TPU v7x, 512 devices: a whole 4x8x8 slice. The times are simulated.
512 devices in a mesh: exp: 128 (over y, z, core), hid: 4 (over x).
Axes of the slice: x: 4, y: 8, z: 8, core: 2. Of those that a mesh axis runs over, the one named last changes fastest.
Arguments:
- tokens: bfloat16 [4096, 4096], P('exp', 'hid'), may hold values from -6 to 6
- expert_ids: int32 [4096, 8], P('exp'), may hold values from 0 to 127, all different within a row; in each aligned block of 16 rows (0 to 15, 16 to 31, ...) at most 2 rows name the same one
- combine: float32 [4096, 8], P('exp'), may hold values from 0.05 to 0.4
- sign_bits: int32 [128, 768], P('exp'), may hold values from 0 to 1
- w_gate: bfloat16 [128, 768, 4096], P('exp', 'hid'), may hold values from -0.09375 to 0.09375
- w_up: bfloat16 [128, 768, 4096], P('exp', 'hid'), may hold values from -0.09375 to 0.09375
- w_down: bfloat16 [128, 768, 4096], P('exp', 'hid'), may hold values from -0.21875 to 0.21875
Outputs:
- next_input: bfloat16 [4096, 4096], P('exp', 'hid')
- hessian: bfloat16 [128, 768, 768], P('exp', 'hid')
Inputs may be any that keep to these rules, and one draw needn't show every extreme that they name: `expert_ids`: each row names 8 different experts. Within each aligned block of 16 rows (one micro-batch of one index of exp) no expert is named by more than 2 rows, a bound that some block reaches. `sign_bits`: 0 stands for the sign -1, 1 for +1.
All inputs are finite; a program needn't handle non-finite values.
Results may differ from a plain program's by a relative error of at most 0.0065.
Values may be sent and summed in bfloat16 or wider, within the bound.
No kernel may reach another device: no remote copies, remote signals or barrier semaphores. Data moves between devices by JAX's collectives and lax.ppermute only.
A program may use at most 64 MiB of HBM per device.

v0:
```python
import jax
import jax.numpy as jnp
import numpy as np
from jax import lax
from jax.sharding import PartitionSpec as P


def paley_twelve():
    residues = set((number * number % 11 for number in range(1, 11)))
    legendre = [0] + [1 if number in residues else -1 for number in range(1, 11)]
    hadamard = np.zeros((12, 12))
    hadamard[0, 1:] = 1.0
    hadamard[1:, 0] = -1.0
    for row_index in range(11):
        for col_index in range(11):
            hadamard[row_index + 1, col_index + 1] = legendre[(col_index - row_index) % 11]
    return hadamard + np.eye(12)


def sylvester(order_size):
    positions = jnp.arange(order_size, dtype=jnp.int32)
    common = positions[:, None] & positions[None, :]
    parity = jnp.zeros_like(common)
    for bit_pos in range(order_size.bit_length()):
        parity = parity + (common >> bit_pos & 1)
    return (1 - 2 * (parity % 2)).astype(jnp.float32)


def rotate(hidden, sign_rows, paley_table, sylvester_table):
    values = hidden.astype(jnp.float32) * jnp.expand_dims(sign_rows, -2)
    blocks = values.reshape(values.shape[:-1] + (12, sylvester_table.shape[0]))
    turned = jnp.einsum(
        "...ab,ca,db->...cd", blocks, paley_table, sylvester_table, precision=lax.Precision.HIGHEST
    )
    return turned.reshape(values.shape)


def rank_of_pick(ids_block, experts):
    flat_ids = ids_block.reshape(-1)
    onehot = (flat_ids[:, None] == jnp.arange(experts, dtype=jnp.int32)[None, :]).astype(jnp.int32)
    before = jnp.cumsum(onehot, axis=0) - onehot
    return jnp.sum(before * onehot, axis=1).reshape(ids_block.shape)


def local(tokens, expert_ids, combine, sign_bits, w_gate, w_up, w_down):
    n_exp = lax.axis_size("exp")
    n_hid = lax.axis_size("hid")
    hid_index = lax.axis_index("hid")
    local_experts = w_gate.shape[0]
    experts = local_experts * n_exp
    tok_rows = tokens.shape[0]
    own_cols = tokens.shape[1]
    half_rows = tok_rows // 2
    top_count = expert_ids.shape[1]
    capacity = min(half_rows, max(2, 2 * half_rows * top_count // experts))
    hidden_units = sign_bits.shape[1]
    share_rows = hidden_units // n_hid
    slot_count = n_exp * capacity
    paley_table = jnp.asarray(paley_twelve(), jnp.float32)
    sylvester_table = sylvester(hidden_units // 12)
    sign_rows = (2 * sign_bits - 1).astype(jnp.float32)
    gram_scale = experts / (tok_rows * n_exp * top_count * hidden_units)
    whole_rows = lax.all_gather(tokens, "hid", axis=1, tiled=True)
    gram_total = jnp.zeros((local_experts, share_rows, hidden_units), jnp.float32)
    results = []
    for batch_index in range(2):
        first_row = batch_index * half_rows
        ids_block = expert_ids[first_row : first_row + half_rows]
        picks_rank = rank_of_pick(ids_block, experts)
        target = ids_block * capacity + picks_rank
        selector = jnp.any(
            target[None, :, :] == jnp.arange(experts * capacity, dtype=jnp.int32)[:, None, None],
            axis=2,
        ).astype(jnp.bfloat16)
        sending = jnp.dot(
            selector,
            whole_rows[first_row : first_row + half_rows],
            preferred_element_type=jnp.float32,
        ).astype(jnp.bfloat16)
        arrived = lax.all_to_all(sending, "exp", split_axis=0, concat_axis=0, tiled=True)
        row_width = arrived.shape[1]
        expert_in = arrived.reshape(n_exp, local_experts, capacity, row_width).transpose(1, 0, 2, 3)
        expert_in = expert_in.reshape(local_experts, slot_count, row_width)
        gate_act = jnp.einsum("esd,efd->esf", expert_in, w_gate, preferred_element_type=jnp.float32)
        up_act = jnp.einsum("esd,efd->esf", expert_in, w_up, preferred_element_type=jnp.float32)
        hidden = (jax.nn.silu(gate_act) * up_act).astype(jnp.bfloat16)
        full_hidden = lax.all_gather(hidden, "hid", axis=2, tiled=True)
        partial_value = jnp.einsum(
            "esf,efd->esd", hidden, w_down, preferred_element_type=jnp.float32
        )
        partial_value = lax.optimization_barrier(partial_value.astype(jnp.bfloat16)).astype(
            jnp.float32
        )
        summed = lax.psum_scatter(
            partial_value.astype(jnp.bfloat16), "hid", scatter_dimension=2, tiled=True
        )
        outgoing = summed.reshape(local_experts, n_exp, capacity, own_cols).transpose(1, 0, 2, 3)
        outgoing = outgoing.reshape(n_exp * local_experts * capacity, own_cols)
        back_rows = lax.all_to_all(outgoing, "exp", split_axis=0, concat_axis=0, tiled=True)
        picked = back_rows[target]
        weights = combine[first_row : first_row + half_rows]
        mixed_rows = tokens[first_row : first_row + half_rows].astype(jnp.float32) + jnp.sum(
            weights[:, :, None] * picked.astype(jnp.float32), axis=1
        )
        results.append(mixed_rows.astype(jnp.bfloat16))
        rotated = rotate(full_hidden, sign_rows, paley_table, sylvester_table)
        own_rotated = lax.dynamic_slice_in_dim(rotated, hid_index * share_rows, share_rows, 2)
        gram_total = gram_total + jnp.einsum(
            "esi,esj->eij", own_rotated, rotated, precision=lax.Precision.HIGHEST
        )
    hessian = (gram_total * gram_scale).astype(jnp.bfloat16)
    return (jnp.concatenate(results, axis=0), hessian)


def solution(mesh):
    placed = (
        P("exp", "hid"),
        P("exp", None),
        P("exp", None),
        P("exp", None),
        P("exp", "hid", None),
        P("exp", "hid", None),
        P("exp", "hid", None),
    )
    return jax.shard_map(
        local,
        mesh=mesh,
        in_specs=placed,
        out_specs=(P("exp", "hid"), P("exp", "hid", None)),
        check_vma=False,
    )
```

profile of v0, /device:TPU:1, one launch (start us, length us, event | category | flops | bytes accessed | tf_op | source)
XLA Modules:
  0.0 254.5 jit_solution(1485017217587112632)
XLA Ops:
  7.2 0.9 fusion.86
  8.1 0.1 eq.65
  8.2 0.1 fusion.46
  8.3 0.2 reduce_window_sum.18
  8.5 0.2 select_reduce_fusion
  8.8 0.1 fusion.45
  8.9 10.7 %all_gather.9 = bf16[32,4096]{1,0:T(8,128)(2,1)S(1)} all-gather(bf16[32,1024]{1,0:T(8,128)(2,1)} %param.8), channel_id=1, replica_groups=mesh['exp'=128,'hid'=4] {'hid'}, dimensions={1}, use_global_device_ids=true | all-gather | bytes 327680 | tf_op jit(solution)/shard_map/all_gather | solution.py:63
  19.7 2.1 convolution_convert_fusion.1
  21.8 4.4 %all_to_all.38 = bf16[128,2,4096]{2,1,0:T(2,128)(2,1)} reshape(bf16[256,4096]{1,0:T(8,128)(2,1)} %convolution_convert_fusion.1) | data formatting | bytes 4194304 | tf_op jit(solution)/shard_map/all_to_all | solution.py:80
  26.2 20.9 %all-to-all-start.2 = ((bf16[128,2,4096]{2,1,0:T(2,128)(2,1)}), bf16[128,2,4096]{2,1,0:T(2,128)(2,1)}, u32[]{:S(2)}, u32[]{:S(2)}) async-start(bf16[128,2,4096]{2,1,0:T(2,128)(2,1)} %all_to_all.38), calls=%async_computation.3 | async-start | bytes 4194304 | tf_op jit(solution)/shard_map/all_to_all | solution.py:80
  47.2 0.1 eq.58
  47.3 0.1 fusion.47
  47.4 0.2 reduce_window_sum.17
  47.5 0.2 select_reduce_fusion.1
  47.8 0.1 fusion.44
  48.0 2.1 convolution_convert_fusion.3
  50.0 4.4 %all_to_all.32 = bf16[128,2,4096]{2,1,0:T(2,128)(2,1)} reshape(bf16[256,4096]{1,0:T(8,128)(2,1)} %convolution_convert_fusion.3) | data formatting | bytes 4194304 | tf_op jit(solution)/shard_map/all_to_all | solution.py:80
  54.4 44.5 %all-to-all-done.2 = bf16[128,2,4096]{2,1,0:T(2,128)(2,1)} async-done(((bf16[128,2,4096]{2,1,0:T(2,128)(2,1)}), bf16[128,2,4096]{2,1,0:T(2,128)(2,1)}, u32[]{:S(2)}, u32[]{:S(2)}) %all-to-all-start.2) | async-done | bytes 2097184 | tf_op jit(solution)/shard_map/all_to_all | solution.py:80
  98.9 8.2 %all-to-all-start = ((bf16[128,2,4096]{2,1,0:T(2,128)(2,1)}), bf16[128,2,4096]{2,1,0:T(2,128)(2,1)}, u32[]{:S(2)}, u32[]{:S(2)}) async-start(bf16[128,2,4096]{2,1,0:T(2,128)(2,1)} %all_to_all.32), calls=%async_computation | async-start | bytes 4194304 | tf_op jit(solution)/shard_map/all_to_all | solution.py:80
  107.1 4.2 %all_to_all.40 = bf16[256,4096]{1,0:T(8,128)(2,1)} reshape(bf16[128,2,4096]{2,1,0:T(2,128)(2,1)} %all-to-all-done.2) | data formatting | bytes 4194304 | tf_op jit(solution)/shard_map/all_to_all | solution.py:80
  111.4 2.6 %fusion.8 = f32[256,192]{0,1:T(8,128)S(1)} fusion(bf16[256,4096]{1,0:T(8,128)(2,1)} %all_to_all.40, bf16[1,192,4096]{2,1,0:T(8,128)(2,1)S(1)} %copy-done.3), kind=kOutput, calls=%fused_computation.14 | convolution fusion | flops 402653184 | bytes 3866624 | tf_op jit(solution)/shard_map/esd,efd->esf/dot_general | solution.py:84
  114.1 0.8 fusion.21
  114.9 2.1 fusion.1
  117.1 41.8 %all-to-all-done = bf16[128,2,4096]{2,1,0:T(2,128)(2,1)} async-done(((bf16[128,2,4096]{2,1,0:T(2,128)(2,1)}), bf16[128,2,4096]{2,1,0:T(2,128)(2,1)}, u32[]{:S(2)}, u32[]{:S(2)}) %all-to-all-start) | async-done | bytes 2097184 | tf_op jit(solution)/shard_map/all_to_all | solution.py:80
  158.9 4.1 %all_to_all.34 = bf16[256,4096]{1,0:T(8,128)(2,1)} reshape(bf16[128,2,4096]{2,1,0:T(2,128)(2,1)} %all-to-all-done) | data formatting | bytes 4194304 | tf_op jit(solution)/shard_map/all_to_all | solution.py:80
  163.0 2.6 %fusion.10 = f32[256,192]{0,1:T(8,128)S(1)} fusion(bf16[256,4096]{1,0:T(8,128)(2,1)} %all_to_all.34, bf16[1,192,4096]{2,1,0:T(8,128)(2,1)S(1)} %copy-done.3), kind=kOutput, calls=%fused_computation.16 | convolution fusion | flops 402653184 | bytes 3866624 | tf_op jit(solution)/shard_map/esd,efd->esf/dot_general | solution.py:84
  165.7 0.9 fusion.24
  166.5 2.1 fusion
  169.1 2.0 all_to_all.41
  171.1 8.3 %all-to-all-start.3 = ((bf16[128,2,1024]{2,1,0:T(2,128)(2,1)}), bf16[128,2,1024]{2,1,0:T(2,128)(2,1)}, u32[]{:S(2)}, u32[]{:S(2)}) async-start(bf16[128,2,1024]{2,1,0:T(2,128)(2,1)} %all_to_all.41), calls=%async_computation.5 | async-start | bytes 1048576 | tf_op jit(solution)/shard_map/all_to_all | solution.py:99
  179.4 13.0 %all-gather.1 = bf16[256,768]{0,1:T(8,128)(2,1)S(1)} all-gather(bf16[256,192]{0,1:T(8,128)(2,1)S(1)} %fusion.21), channel_id=3, replica_groups=mesh['exp'=128,'hid'=4] {'hid'}, dimensions={1}, use_global_device_ids=true | all-gather | bytes 491520 | tf_op jit(solution)/shard_map/all_gather | solution.py:87
  192.4 12.0 %all-gather = bf16[256,768]{0,1:T(8,128)(2,1)S(1)} all-gather(bf16[256,192]{0,1:T(8,128)(2,1)S(1)} %fusion.24), channel_id=2, replica_groups=mesh['exp'=128,'hid'=4] {'hid'}, dimensions={1}, use_global_device_ids=true | all-gather | bytes 491520 | tf_op jit(solution)/shard_map/all_gather | solution.py:87
  204.4 0.2 convert_multiply_fusion
  204.6 1.4 fusion.29
  206.0 2.0 all_to_all.35
  208.0 17.4 %all-to-all-start.1 = ((bf16[128,2,1024]{2,1,0:T(2,128)(2,1)}), bf16[128,2,1024]{2,1,0:T(2,128)(2,1)}, u32[]{:S(2)}, u32[]{:S(2)}) async-start(bf16[128,2,1024]{2,1,0:T(2,128)(2,1)} %all_to_all.35), calls=%async_computation.2 | async-start | bytes 1048576 | tf_op jit(solution)/shard_map/all_to_all | solution.py:99
  225.5 1.3 fusion.33
  226.8 0.9 fusion.38
  227.7 1.4 fusion.27
  229.1 1.3 fusion.31
  230.4 1.7 fusion.14
  232.1 1.2 all_to_all.43
  233.3 0.9 gather_fusion.1
  234.2 10.3 %all-to-all-done.1 = bf16[128,2,1024]{2,1,0:T(2,128)(2,1)} async-done(((bf16[128,2,1024]{2,1,0:T(2,128)(2,1)}), bf16[128,2,1024]{2,1,0:T(2,128)(2,1)}, u32[]{:S(2)}, u32[]{:S(2)}) %all-to-all-start.1) | async-done | bytes 524320 | tf_op jit(solution)/shard_map/all_to_all | solution.py:99
  244.5 1.2 all_to_all.37
  245.8 0.9 gather_fusion
  246.6 0.4 fusion.35
  247.0 0.6 pad_maximum_fusion
  (42 shorter events, 1.1 us)
Async XLA Ops:
  7.2 107.8 %copy-start = (bf16[1,192,4096]{2,1,0:T(8,128)(2,1)S(1)}, bf16[1,192,4096]{2,1,0:T(8,128)(2,1)}, u32[]{:S(2)}) copy-start(bf16[1,192,4096]{2,1,0:T(8,128)(2,1)} %param.14) | copy-start | bytes 4718596
  26.2 72.7 %all-to-all-start.2 = ((bf16[128,2,4096]{2,1,0:T(2,128)(2,1)}), bf16[128,2,4096]{2,1,0:T(2,128)(2,1)}, u32[]{:S(2)}, u32[]{:S(2)}) async-start(bf16[128,2,4096]{2,1,0:T(2,128)(2,1)} %all_to_all.38), calls=%async_computation.3 | async-start | bytes 4194304 | tf_op jit(solution)/shard_map/all_to_all | solution.py:80
  98.9 60.0 %all-to-all-start = ((bf16[128,2,4096]{2,1,0:T(2,128)(2,1)}), bf16[128,2,4096]{2,1,0:T(2,128)(2,1)}, u32[]{:S(2)}, u32[]{:S(2)}) async-start(bf16[128,2,4096]{2,1,0:T(2,128)(2,1)} %all_to_all.32), calls=%async_computation | async-start | bytes 4194304 | tf_op jit(solution)/shard_map/all_to_all | solution.py:80
  107.1 4.3 %copy-start.3 = (bf16[1,192,4096]{2,1,0:T(8,128)(2,1)S(1)}, bf16[1,192,4096]{2,1,0:T(8,128)(2,1)}, u32[]{:S(2)}) copy-start(bf16[1,192,4096]{2,1,0:T(8,128)(2,1)} %param.12) | copy-start | bytes 4718596
  107.1 62.0 %reduce-scatter.5.cloned.1.call-start = ((), (), s32[]{:S(2)}) async-start(), calls=%async_computation.7 | async-start | bytes 2621440 | tf_op jit(solution)/shard_map/reduce_scatter | solution.py:94
  111.4 2.6 %copy-start.1 = (bf16[256,4096]{1,0:T(8,128)(2,1)S(1)}, bf16[256,4096]{1,0:T(8,128)(2,1)}, u32[]{:S(2)}) copy-start(bf16[256,4096]{1,0:T(8,128)(2,1)} %all_to_all.40) | copy-start | bytes 6291460
  111.4 2.7 %copy-start.8 = (bf16[1,192,4096]{2,1,0:T(8,128)(2,1)S(1)}, bf16[1,192,4096]{2,1,0:T(8,128)(2,1)}, u32[]{:S(2)}) copy-start(bf16[1,192,4096]{2,1,0:T(8,128)(2,1)} %param.13) | copy-start | bytes 4718596
  117.0 89.0 %reduce-scatter.3.cloned.1.call-start = ((), (), s32[]{:S(2)}) async-start(), calls=%async_computation.6 | async-start | bytes 2621440 | tf_op jit(solution)/shard_map/reduce_scatter | solution.py:94
  163.0 2.6 %copy-start.2 = (bf16[256,4096]{1,0:T(8,128)(2,1)S(1)}, bf16[256,4096]{1,0:T(8,128)(2,1)}, u32[]{:S(2)}) copy-start(bf16[256,4096]{1,0:T(8,128)(2,1)} %all_to_all.34) | copy-start | bytes 6291460
  163.0 2.7 %copy-start.9 = (bf16[1,192,4096]{2,1,0:T(8,128)(2,1)S(1)}, bf16[1,192,4096]{2,1,0:T(8,128)(2,1)}, u32[]{:S(2)}) copy-start(bf16[1,192,4096]{2,1,0:T(8,128)(2,1)} %param.13) | copy-start | bytes 4718596
  166.5 2.2 copy-start.6
  168.6 10.8 %copy-start.7 = (s32[1,768]{1,0:T(1,128)S(1)}, s32[1,768]{1,0:T(1,128)}, u32[]{:S(2)}) copy-start(s32[1,768]{1,0:T(1,128)} %param.11) | copy-start | bytes 9220
  171.1 33.5 %copy-start.5 = (f32[12,12,1]{1,0,2:T(8,128)S(1)}, f32[12,12,1]{1,0,2:T(8,128)}, u32[]{:S(2)}) copy-start(f32[12,12,1]{1,0,2:T(8,128)} %constant.69) | copy-start | bytes 1732
  171.1 37.0 %all-to-all-start.3 = ((bf16[128,2,1024]{2,1,0:T(2,128)(2,1)}), bf16[128,2,1024]{2,1,0:T(2,128)(2,1)}, u32[]{:S(2)}, u32[]{:S(2)}) async-start(bf16[128,2,1024]{2,1,0:T(2,128)(2,1)} %all_to_all.41), calls=%async_computation.5 | async-start | bytes 1048576 | tf_op jit(solution)/shard_map/all_to_all | solution.py:99
  208.0 36.5 %all-to-all-start.1 = ((bf16[128,2,1024]{2,1,0:T(2,128)(2,1)}), bf16[128,2,1024]{2,1,0:T(2,128)(2,1)}, u32[]{:S(2)}, u32[]{:S(2)}) async-start(bf16[128,2,1024]{2,1,0:T(2,128)(2,1)} %all_to_all.35), calls=%async_computation.2 | async-start | bytes 1048576 | tf_op jit(solution)/shard_map/all_to_all | solution.py:99
  234.2 12.8 %copy-start.4 = (bf16[32,1024]{1,0:T(8,128)(2,1)S(1)}, bf16[32,1024]{1,0:T(8,128)(2,1)}, u32[]{:S(2)}) copy-start(bf16[32,1024]{1,0:T(8,128)(2,1)} %param.8) | copy-start | bytes 196612
Sparse Core Ops, SparseCore 0:
  117.1 35.1 reduce-scatter.4
  168.8 33.2 reduce-scatter.2
where the time goes:
time: 255 us
  waiting for transfers between devices  96.6 us (38%)
  starting transfers between devices  54.9 us (22%)
  blocking collectives  35.7 us (14%)
  local copies, waits for them, and re-layouts  27.3 us (11%)
  matrix products  23.2 us (9%)
  between operations  14.4 us (6%)
    all_to_all x2, waiting for transfers between devices, local(): lax.all_to_all(sending, 'exp', split_axis=0, concat_axis=0, tiled=True)  86.3 us
    all_to_all x2, starting transfers between devices, local(): lax.all_to_all(sending, 'exp', split_axis=0, concat_axis=0, tiled=True)  29.1 us
    all_to_all x2, starting transfers between devices, local(): lax.all_to_all(outgoing, 'exp', split_axis=0, concat_axis=0, tiled=True)  25.7 us
    all_gather x2, blocking collectives, local(): full_hidden = lax.all_gather(hidden, 'hid', axis=2, tiled=True)  25 us
    all_to_all x4, local copies, waits for them, and re-layouts, local(): lax.all_to_all(sending, 'exp', split_axis=0, concat_axis=0, tiled=True)  17.2 us
    all_gather x1, blocking collectives, local(): whole_rows = lax.all_gather(tokens, 'hid', axis=1, tiled=True)  10.7 us
    all_to_all x2, waiting for transfers between devices, local(): lax.all_to_all(outgoing, 'exp', split_axis=0, concat_axis=0, tiled=True)  10.3 us
    all_to_all x4, local copies, waits for them, and re-layouts, local(): lax.all_to_all(outgoing, 'exp', split_axis=0, concat_axis=0, tiled=True)  6.54 us
  transfers between devices with their start and end apart: 6, of which 3 were waited for; matrix products, arithmetic and copies ran while one was open for 9% of the time, Pallas kernels for 0%

commit v1 on v0

--- a/solution.py
+++ b/solution.py
@@ -49,7 +49,6 @@
     local_experts = w_gate.shape[0]
     experts = local_experts * n_exp
     tok_rows = tokens.shape[0]
-    own_cols = tokens.shape[1]
     half_rows = tok_rows // 2
     top_count = expert_ids.shape[1]
     capacity = min(half_rows, max(2, 2 * half_rows * top_count // experts))
@@ -60,7 +59,7 @@
     sylvester_table = sylvester(hidden_units // 12)
     sign_rows = (2 * sign_bits - 1).astype(jnp.float32)
     gram_scale = experts / (tok_rows * n_exp * top_count * hidden_units)
-    whole_rows = lax.all_gather(tokens, "hid", axis=1, tiled=True)
+    down_cols = lax.all_to_all(w_down, "hid", split_axis=2, concat_axis=1, tiled=True)
     gram_total = jnp.zeros((local_experts, share_rows, hidden_units), jnp.float32)
     results = []
     for batch_index in range(2):
@@ -74,10 +73,11 @@
         ).astype(jnp.bfloat16)
         sending = jnp.dot(
             selector,
-            whole_rows[first_row : first_row + half_rows],
+            tokens[first_row : first_row + half_rows],
             preferred_element_type=jnp.float32,
         ).astype(jnp.bfloat16)
         arrived = lax.all_to_all(sending, "exp", split_axis=0, concat_axis=0, tiled=True)
+        arrived = lax.all_gather(arrived, "hid", axis=1, tiled=True)
         row_width = arrived.shape[1]
         expert_in = arrived.reshape(n_exp, local_experts, capacity, row_width).transpose(1, 0, 2, 3)
         expert_in = expert_in.reshape(local_experts, slot_count, row_width)
@@ -85,17 +85,11 @@
         up_act = jnp.einsum("esd,efd->esf", expert_in, w_up, preferred_element_type=jnp.float32)
         hidden = (jax.nn.silu(gate_act) * up_act).astype(jnp.bfloat16)
         full_hidden = lax.all_gather(hidden, "hid", axis=2, tiled=True)
-        partial_value = jnp.einsum(
-            "esf,efd->esd", hidden, w_down, preferred_element_type=jnp.float32
-        )
-        partial_value = lax.optimization_barrier(partial_value.astype(jnp.bfloat16)).astype(
-            jnp.float32
-        )
-        summed = lax.psum_scatter(
-            partial_value.astype(jnp.bfloat16), "hid", scatter_dimension=2, tiled=True
-        )
-        outgoing = summed.reshape(local_experts, n_exp, capacity, own_cols).transpose(1, 0, 2, 3)
-        outgoing = outgoing.reshape(n_exp * local_experts * capacity, own_cols)
+        summed = jnp.einsum(
+            "esf,efd->esd", full_hidden, down_cols, preferred_element_type=jnp.float32
+        ).astype(jnp.bfloat16)
+        outgoing = summed.reshape(local_experts, n_exp, capacity, -1).transpose(1, 0, 2, 3)
+        outgoing = outgoing.reshape(n_exp * local_experts * capacity, -1)
         back_rows = lax.all_to_all(outgoing, "exp", split_axis=0, concat_axis=0, tiled=True)
         picked = back_rows[target]
         weights = combine[first_row : first_row + half_rows]

time: 255 us -> 256 us (level)
  waiting for transfers between devices: 96.6 us -> 26.7 us
  blocking collectives: 35.7 us -> 84.4 us
  other arithmetic: 2.38 us -> 29 us
  starting transfers between devices: 54.9 us -> 32.8 us
  local copies, waits for them, and re-layouts: 27.3 us -> 48.2 us
  matrix products: 23.2 us -> 19.1 us
    all_to_all x2 -> x1, waiting for transfers between devices: 86.3 us -> 16.4 us  [local(): lax.all_to_all(w_down, 'hid', split_axis=2, concat_axis=1, tiled=True)]
    all_to_all x0 -> x2, blocking collectives: none -> 63.9 us  [local(): lax.all_to_all(sending, 'exp', split_axis=0, concat_axis=0, tiled=True)]
    unnamed x0 -> x1, other arithmetic: none -> 25 us
    all_to_all x2 -> x1, starting transfers between devices: 29.1 us -> 4.14 us  [local(): lax.all_to_all(w_down, 'hid', split_axis=2, concat_axis=1, tiled=True)]
    unnamed x22 -> x34, local copies, waits for them, and re-layouts: 0.3 us -> 20.6 us
    all_to_all x4, local copies, waits for them, and re-layouts: 17.2 us -> 2.41 us  [local(): lax.all_to_all(sending, 'exp', split_axis=0, concat_axis=0, tiled=True)]
    all_to_all x0 -> x3, local copies, waits for them, and re-layouts: none -> 14.1 us  [local(): lax.all_to_all(w_down, 'hid', split_axis=2, concat_axis=1, tiled=True)]
    all_gather x1 -> x0, blocking collectives: 10.7 us -> none  [local(): whole_rows = lax.all_gather(tokens, 'hid', axis=1, tiled=True)]
  transfers between devices with their start and end apart: 6 -> 5, of which waited for: 3 -> 2; matrix products, arithmetic and copies ran while one was open for 9% -> 31% of each run, Pallas kernels for 0% -> 0%
where the time goes in v1:
time: 256 us; the launch traced here: 255 us
  blocking collectives  84.4 us (33%)
  local copies, waits for them, and re-layouts  48.2 us (19%)
  starting transfers between devices  32.8 us (13%)
  other arithmetic  29 us (11%)
  waiting for transfers between devices  26.7 us (10%)
  matrix products  19.1 us (7%)
  between operations  14.4 us (6%)
    all_to_all x2, blocking collectives, local(): lax.all_to_all(sending, 'exp', split_axis=0, concat_axis=0, tiled=True)  63.9 us
    all_to_all x2, starting transfers between devices, local(): lax.all_to_all(outgoing, 'exp', split_axis=0, concat_axis=0, tiled=True)  28.6 us
    unnamed x1, other arithmetic  25 us
    unnamed x34, local copies, waits for them, and re-layouts  20.6 us
    all_gather x2, blocking collectives, local(): full_hidden = lax.all_gather(hidden, 'hid', axis=2, tiled=True)  20.5 us
    all_to_all x1, waiting for transfers between devices, local(): lax.all_to_all(w_down, 'hid', split_axis=2, concat_axis=1, tiled=True)  16.4 us
    all_to_all x3, local copies, waits for them, and re-layouts, local(): lax.all_to_all(w_down, 'hid', split_axis=2, concat_axis=1, tiled=True)  14.1 us
    all_to_all x2, waiting for transfers between devices, local(): lax.all_to_all(outgoing, 'exp', split_axis=0, concat_axis=0, tiled=True)  10.3 us
  transfers between devices with their start and end apart: 5, of which 2 were waited for; matrix products, arithmetic and copies ran while one was open for 31% of the time, Pallas kernels for 0%

profile of v1, /device:TPU:1, one launch (start us, length us, event | category | flops | bytes accessed | tf_op | source)
XLA Modules:
  0.0 254.6 jit_solution(8127304555894847153)
XLA Ops:
  7.2 0.9 fusion.82
  9.0 1.1 convolution_convert_fusion.1
  10.3 37.8 %all_to_all.63 = bf16[128,2,1024]{2,1,0:T(2,128)(2,1)S(1)} all-to-all(bf16[128,2,1024]{2,1,0:T(2,128)(2,1)S(1)} %all_to_all.52), channel_id=1, replica_groups=mesh['exp'=128,'hid'=4] {'exp'}, dimensions={0} | all-to-all | bytes 1048576 | tf_op jit(solution)/shard_map/all_to_all | solution.py:79
  48.0 1.0 all_to_all.54
  50.0 0.3 convolution_convert_fusion.3
  50.3 0.2 all_to_all.43
  50.5 26.2 %all_to_all.64 = bf16[128,2,1024]{2,1,0:T(2,128)(2,1)S(1)} all-to-all(bf16[128,2,1024]{2,1,0:T(2,128)(2,1)S(1)} %all_to_all.43), channel_id=1, replica_groups=mesh['exp'=128,'hid'=4] {'exp'}, dimensions={0} | all-to-all | bytes 1048576 | tf_op jit(solution)/shard_map/all_to_all | solution.py:79
  76.7 1.0 all_to_all.45
  77.7 9.9 %copy.40 = bf16[1,192,4096]{1,0,2:T(2,128)(2,1)} copy(bf16[1,192,4096]{2,1,0:T(8,128)(2,1)} %param.14) | data formatting | bytes 3145728 | tf_op args[6]
  87.6 0.5 broadcast.82
  88.1 25.0 %reduce.2 = bf16[4096,192]{1,0:T(8,128)(2,1)} reduce(bf16[4096,1,192]{2,1,0:T(2,128)(2,1)} %bitcast.77, bf16[]{:T(256)} %broadcast.82), dimensions={1}, to_apply=%bitcast.61.reduce_sub_computation | reduce | bytes 3145730
  113.1 5.0 %reshape.170 = bf16[4,2,98304]{2,1,0:T(2,128)(2,1)} reshape(bf16[4096,192]{1,0:T(8,128)(2,1)} %reduce.2) | data formatting | bytes 3145728
  118.1 4.1 %all-to-all-start.1 = ((bf16[4,2,98304]{2,1,0:T(2,128)(2,1)}), bf16[4,2,98304]{2,1,0:T(2,128)(2,1)S(1)}, u32[]{:S(2)}, u32[]{:S(2)}) async-start(bf16[4,2,98304]{2,1,0:T(2,128)(2,1)} %reshape.170), calls=%async_computation.1 | async-start | bytes 3145728 | tf_op jit(solution)/shard_map/all_to_all | solution.py:62
  122.4 0.7 copy.43
  123.2 0.7 copy.38
  123.9 0.6 convert_reduce_fusion
  124.5 16.4 %all-to-all-done.1 = bf16[4,2,98304]{2,1,0:T(2,128)(2,1)S(1)} async-done(((bf16[4,2,98304]{2,1,0:T(2,128)(2,1)}), bf16[4,2,98304]{2,1,0:T(2,128)(2,1)S(1)}, u32[]{:S(2)}, u32[]{:S(2)}) %all-to-all-start.1) | async-done | bytes 1572896 | tf_op jit(solution)/shard_map/all_to_all | solution.py:62
  140.9 4.1 %reshape.171 = bf16[4096,1,192]{2,1,0:T(2,128)(2,1)} reshape(bf16[4,2,98304]{2,1,0:T(2,128)(2,1)S(1)} %all-to-all-done.1) | data formatting | bytes 3145728
  145.0 9.6 %copy.41 = bf16[1,192,4096]{2,1,0:T(8,128)(2,1)} copy(bf16[1,192,4096]{1,0,2:T(2,128)(2,1)} %bitcast.78) | data formatting | bytes 3145728 | tf_op jit(solution)/shard_map/all_to_all | solution.py:62
  154.6 2.9 %all_to_all.47 = bf16[1,192,4,1024]{3,2,1,0:T(4,128)(2,1)S(1)} reshape(bf16[1,192,4096]{2,1,0:T(8,128)(2,1)} %copy.41) | data formatting | bytes 3145728 | tf_op jit(solution)/shard_map/all_to_all | solution.py:62
  157.5 1.6 copy.42
  159.1 2.6 %fusion.4 = f32[256,192]{0,1:T(8,128)S(1)} fusion(bf16[256,4096]{1,0:T(8,128)(2,1)} %all-gather.7.cloned.1.call-done, bf16[1,192,4096]{2,1,0:T(8,128)(2,1)S(1)} %copy-done), kind=kOutput, calls=%fused_computation.6 | convolution fusion | flops 402653184 | bytes 3866624 | tf_op jit(solution)/shard_map/esd,efd->esf/dot_general | solution.py:84
  161.8 0.9 fusion.17
  162.7 9.6 %all-gather.1 = bf16[256,768]{0,1:T(8,128)(2,1)S(1)} all-gather(bf16[256,192]{0,1:T(8,128)(2,1)S(1)} %fusion.17), channel_id=3, replica_groups=mesh['exp'=128,'hid'=4] {'hid'}, dimensions={1}, use_global_device_ids=true | all-gather | bytes 491520 | tf_op jit(solution)/shard_map/all_gather | solution.py:87
  172.3 1.4 convolution_convert_fusion
  173.7 2.0 all_to_all.55
  175.7 12.7 %all-to-all-start.4 = ((bf16[128,2,1024]{2,1,0:T(2,128)(2,1)}), bf16[128,2,1024]{2,1,0:T(2,128)(2,1)}, u32[]{:S(2)}, u32[]{:S(2)}) async-start(bf16[128,2,1024]{2,1,0:T(2,128)(2,1)} %all_to_all.55), calls=%async_computation.4 | async-start | bytes 1048576 | tf_op jit(solution)/shard_map/all_to_all | solution.py:93
  188.5 2.6 %fusion.6 = f32[256,192]{0,1:T(8,128)S(1)} fusion(bf16[256,4096]{1,0:T(8,128)(2,1)} %all-gather.5.cloned.1.call-done, bf16[1,192,4096]{2,1,0:T(8,128)(2,1)S(1)} %copy-done), kind=kOutput, calls=%fused_computation.8 | convolution fusion | flops 402653184 | bytes 3866624 | tf_op jit(solution)/shard_map/esd,efd->esf/dot_general | solution.py:84
  191.1 0.8 fusion.20
  192.0 10.8 %all-gather = bf16[256,768]{0,1:T(8,128)(2,1)S(1)} all-gather(bf16[256,192]{0,1:T(8,128)(2,1)S(1)} %fusion.20), channel_id=2, replica_groups=mesh['exp'=128,'hid'=4] {'hid'}, dimensions={1}, use_global_device_ids=true | all-gather | bytes 491520 | tf_op jit(solution)/shard_map/all_gather | solution.py:87
  202.8 0.7 copy-done.4
  203.6 1.4 convolution_convert_fusion.2
  205.0 2.1 all_to_all.49
  207.0 1.2 convert_multiply_fusion
  208.2 1.4 fusion.25
  209.6 15.9 %all-to-all-start.2 = ((bf16[128,2,1024]{2,1,0:T(2,128)(2,1)}), bf16[128,2,1024]{2,1,0:T(2,128)(2,1)}, u32[]{:S(2)}, u32[]{:S(2)}) async-start(bf16[128,2,1024]{2,1,0:T(2,128)(2,1)} %all_to_all.49), calls=%async_computation.2 | async-start | bytes 1048576 | tf_op jit(solution)/shard_map/all_to_all | solution.py:93
  225.5 1.3 fusion.29
  226.8 0.9 fusion.34
  227.8 1.4 fusion.23
  229.2 1.3 fusion.27
  230.5 1.7 fusion.10
  232.1 1.2 all_to_all.57
  233.4 0.9 gather_fusion.1
  234.3 10.3 %all-to-all-done.2 = bf16[128,2,1024]{2,1,0:T(2,128)(2,1)} async-done(((bf16[128,2,1024]{2,1,0:T(2,128)(2,1)}), bf16[128,2,1024]{2,1,0:T(2,128)(2,1)}, u32[]{:S(2)}, u32[]{:S(2)}) %all-to-all-start.2) | async-done | bytes 524320 | tf_op jit(solution)/shard_map/all_to_all | solution.py:93
  244.6 1.2 all_to_all.51
  245.8 0.9 gather_fusion
  246.7 0.4 fusion.31
  247.1 0.6 pad_maximum_fusion
  (57 shorter events, 2.4 us)
Async XLA Ops:
  7.2 152.0 %copy-start = (bf16[1,192,4096]{2,1,0:T(8,128)(2,1)S(1)}, bf16[1,192,4096]{2,1,0:T(8,128)(2,1)}, u32[]{:S(2)}) copy-start(bf16[1,192,4096]{2,1,0:T(8,128)(2,1)} %param.12) | copy-start | bytes 4718596
  7.2 151.9 %all-gather.7.cloned.1.call-start = ((), (), s32[]{:S(2)}) async-start(), calls=%async_computation.6 | async-start | bytes 2621440 | tf_op jit(solution)/shard_map/all_gather | solution.py:80
  10.3 39.7 %copy-start.5 = (bf16[32,1024]{1,0:T(8,128)(2,1)S(1)}, bf16[32,1024]{1,0:T(8,128)(2,1)}, u32[]{:S(2)}) copy-start(bf16[32,1024]{1,0:T(8,128)(2,1)} %param.8) | copy-start | bytes 196612
  49.1 139.4 %all-gather.5.cloned.1.call-start = ((), (), s32[]{:S(2)}) async-start(), calls=%async_computation.5 | async-start | bytes 2621440 | tf_op jit(solution)/shard_map/all_gather | solution.py:80
  118.1 4.2 %copy-start.10 = (f32[32,8]{0,1:T(8,128)S(1)}, f32[32,8]{0,1:T(8,128)}, u32[]{:S(2)}) copy-start(f32[32,8]{0,1:T(8,128)} %param.10) | copy-start | bytes 3076
  118.1 5.8 %copy-start.11 = (s32[1,768]{1,0:T(1,128)S(1)}, s32[1,768]{1,0:T(1,128)}, u32[]{:S(2)}) copy-start(s32[1,768]{1,0:T(1,128)} %param.11) | copy-start | bytes 9220
  118.1 22.8 %all-to-all-start.1 = ((bf16[4,2,98304]{2,1,0:T(2,128)(2,1)}), bf16[4,2,98304]{2,1,0:T(2,128)(2,1)S(1)}, u32[]{:S(2)}, u32[]{:S(2)}) async-start(bf16[4,2,98304]{2,1,0:T(2,128)(2,1)} %reshape.170), calls=%async_computation.1 | async-start | bytes 3145728 | tf_op jit(solution)/shard_map/all_to_all | solution.py:62
  159.1 2.6 %copy-start.1 = (bf16[256,4096]{1,0:T(8,128)(2,1)S(1)}, bf16[256,4096]{1,0:T(8,128)(2,1)}, u32[]{:S(2)}) copy-start(bf16[256,4096]{1,0:T(8,128)(2,1)} %all-gather.7.cloned.1.call-done) | copy-start | bytes 6291460
  159.1 2.7 %copy-start.12 = (bf16[1,192,4096]{2,1,0:T(8,128)(2,1)S(1)}, bf16[1,192,4096]{2,1,0:T(8,128)(2,1)}, u32[]{:S(2)}) copy-start(bf16[1,192,4096]{2,1,0:T(8,128)(2,1)} %param.13) | copy-start | bytes 4718596
  161.8 10.5 %copy-start.3 = (bf16[1,4,192,1024]{3,2,1,0:T(8,128)(2,1)S(1)}, bf16[1,4,192,1024]{3,2,1,0:T(8,128)(2,1)}, u32[]{:S(2)}) copy-start(bf16[1,4,192,1024]{3,2,1,0:T(8,128)(2,1)} %copy.42) | copy-start | bytes 4718596
  175.7 33.9 %all-to-all-start.4 = ((bf16[128,2,1024]{2,1,0:T(2,128)(2,1)}), bf16[128,2,1024]{2,1,0:T(2,128)(2,1)}, u32[]{:S(2)}, u32[]{:S(2)}) async-start(bf16[128,2,1024]{2,1,0:T(2,128)(2,1)} %all_to_all.55), calls=%async_computation.4 | async-start | bytes 1048576 | tf_op jit(solution)/shard_map/all_to_all | solution.py:93
  188.5 2.6 %copy-start.2 = (bf16[256,4096]{1,0:T(8,128)(2,1)S(1)}, bf16[256,4096]{1,0:T(8,128)(2,1)}, u32[]{:S(2)}) copy-start(bf16[256,4096]{1,0:T(8,128)(2,1)} %all-gather.5.cloned.1.call-done) | copy-start | bytes 6291460
  188.5 2.7 %copy-start.13 = (bf16[1,192,4096]{2,1,0:T(8,128)(2,1)S(1)}, bf16[1,192,4096]{2,1,0:T(8,128)(2,1)}, u32[]{:S(2)}) copy-start(bf16[1,192,4096]{2,1,0:T(8,128)(2,1)} %param.13) | copy-start | bytes 4718596
  202.8 0.7 copy-start.4
  204.9 3.3 %copy-start.7 = (f32[12,12,1]{1,0,2:T(8,128)S(1)}, f32[12,12,1]{1,0,2:T(8,128)}, u32[]{:S(2)}) copy-start(f32[12,12,1]{1,0,2:T(8,128)} %constant.69) | copy-start | bytes 1732
  209.6 35.0 %all-to-all-start.2 = ((bf16[128,2,1024]{2,1,0:T(2,128)(2,1)}), bf16[128,2,1024]{2,1,0:T(2,128)(2,1)}, u32[]{:S(2)}, u32[]{:S(2)}) async-start(bf16[128,2,1024]{2,1,0:T(2,128)(2,1)} %all_to_all.49), calls=%async_computation.2 | async-start | bytes 1048576 | tf_op jit(solution)/shard_map/all_to_all | solution.py:93
  234.2 12.4 %copy-start.8 = (f32[16,8]{1,0:T(8,128)S(1)}, f32[16,8]{1,0:T(8,128)}, u32[]{:S(2)}) copy-start(f32[16,8]{1,0:T(8,128)} %copy.43) | copy-start | bytes 1540
  234.3 12.4 %copy-start.9 = (f32[16,8]{1,0:T(8,128)S(1)}, f32[16,8]{1,0:T(8,128)}, u32[]{:S(2)}) copy-start(f32[16,8]{1,0:T(8,128)} %copy.38) | copy-start | bytes 1540
  245.8 1.3 copy-start.6
Sparse Core Ops, SparseCore 0:
  49.2 29.5 all-gather.6
  80.8 36.1 all-gather.4

commit v2 on v1

v2 whole, which is shorter than its diff:
```python
import jax
import jax.numpy as jnp
import numpy as np
from jax import lax
from jax.sharding import PartitionSpec as P


def paley_twelve():
    residues = set((number * number % 11 for number in range(1, 11)))
    legendre = [0] + [1 if number in residues else -1 for number in range(1, 11)]
    hadamard = np.zeros((12, 12))
    hadamard[0, 1:] = 1.0
    hadamard[1:, 0] = -1.0
    for row_index in range(11):
        for col_index in range(11):
            hadamard[row_index + 1, col_index + 1] = legendre[(col_index - row_index) % 11]
    return hadamard + np.eye(12)


def sylvester(order_size):
    positions = jnp.arange(order_size, dtype=jnp.int32)
    common = positions[:, None] & positions[None, :]
    parity = jnp.zeros_like(common)
    for bit_pos in range(order_size.bit_length()):
        parity = parity + (common >> bit_pos & 1)
    return (1 - 2 * (parity % 2)).astype(jnp.float32)


def rotate(hidden, sign_rows, paley_table, sylvester_table):
    values = hidden.astype(jnp.float32) * jnp.expand_dims(sign_rows, -2)
    blocks = values.reshape(values.shape[:-1] + (12, sylvester_table.shape[0]))
    turned = jnp.einsum(
        "...ab,ca,db->...cd", blocks, paley_table, sylvester_table, precision=lax.Precision.HIGHEST
    )
    return turned.reshape(values.shape)


def rank_of_pick(ids_block, experts):
    flat_ids = ids_block.reshape(-1)
    onehot = (flat_ids[:, None] == jnp.arange(experts, dtype=jnp.int32)[None, :]).astype(jnp.int32)
    before = jnp.cumsum(onehot, axis=0) - onehot
    return jnp.sum(before * onehot, axis=1).reshape(ids_block.shape)


def local(tokens, expert_ids, combine, sign_bits, w_gate, w_up, w_down):
    n_exp = lax.axis_size("exp")
    n_hid = lax.axis_size("hid")
    hid_index = lax.axis_index("hid")
    experts = w_gate.shape[0] * n_exp
    tok_rows, own_cols = tokens.shape
    half_rows = tok_rows // 2
    top_count = expert_ids.shape[1]
    capacity = min(half_rows, max(2, 2 * half_rows * top_count // experts))
    hidden_units = sign_bits.shape[1]
    share_rows = hidden_units // n_hid
    per_pair = 2 * capacity
    paley_table = jnp.asarray(paley_twelve(), jnp.float32)
    sylvester_table = sylvester(hidden_units // 12)
    sign_rows = (2 * sign_bits - 1).astype(jnp.float32)
    gram_scale = experts / (tok_rows * n_exp * top_count * hidden_units)
    down_parts = w_down[0].reshape(share_rows, n_hid, own_cols).transpose(1, 0, 2)
    down_cols = lax.all_to_all(down_parts, "hid", split_axis=0, concat_axis=0, tiled=True)
    down_cols = down_cols.reshape(hidden_units, own_cols)
    ranks = jnp.concatenate(
        [rank_of_pick(expert_ids[b * half_rows : (b + 1) * half_rows], experts) for b in range(2)],
        axis=0,
    )
    batch_of_row = (jnp.arange(tok_rows, dtype=jnp.int32) // half_rows)[:, None]
    target = expert_ids * per_pair + batch_of_row * capacity + ranks
    selector = jnp.any(
        target[None, :, :] == jnp.arange(experts * per_pair, dtype=jnp.int32)[:, None, None],
        axis=2,
    ).astype(jnp.bfloat16)
    sending = jnp.dot(selector, tokens, preferred_element_type=jnp.float32).astype(jnp.bfloat16)
    arrived = lax.all_to_all(sending, "exp", split_axis=0, concat_axis=0, tiled=True)
    expert_in = lax.all_gather(arrived, "hid", axis=1, tiled=True)
    gate_act = jnp.dot(expert_in, w_gate[0].T, preferred_element_type=jnp.float32)
    up_act = jnp.dot(expert_in, w_up[0].T, preferred_element_type=jnp.float32)
    hidden = (jax.nn.silu(gate_act) * up_act).astype(jnp.bfloat16)
    full_hidden = lax.all_gather(hidden, "hid", axis=1, tiled=True)
    out_cols = jnp.dot(full_hidden, down_cols, preferred_element_type=jnp.float32).astype(
        jnp.bfloat16
    )
    back_rows = lax.all_to_all(out_cols, "exp", split_axis=0, concat_axis=0, tiled=True)
    picked = back_rows[target]
    mixed_rows = tokens.astype(jnp.float32) + jnp.sum(
        combine[:, :, None] * picked.astype(jnp.float32), axis=1
    )
    rotated = rotate(full_hidden, sign_rows[0], paley_table, sylvester_table)
    own_rotated = lax.dynamic_slice_in_dim(rotated, hid_index * share_rows, share_rows, 1)
    gram = jnp.dot(own_rotated.T, rotated, precision=lax.Precision.HIGHEST)
    hessian = (gram * gram_scale).astype(jnp.bfloat16)
    return (mixed_rows.astype(jnp.bfloat16), hessian[None])


def solution(mesh):
    placed = (
        P("exp", "hid"),
        P("exp", None),
        P("exp", None),
        P("exp", None),
        P("exp", "hid", None),
        P("exp", "hid", None),
        P("exp", "hid", None),
    )
    return jax.shard_map(
        local,
        mesh=mesh,
        in_specs=placed,
        out_specs=(P("exp", "hid"), P("exp", "hid", None)),
        check_vma=False,
    )
```

time: 256 us -> 199 us (0.78)
  waiting for transfers between devices: 26.7 us -> 76.6 us
  local copies, waits for them, and re-layouts: 48.2 us -> 12.7 us
  other arithmetic: 29 us -> 3.08 us
  blocking collectives: 84.4 us -> 59.3 us
  starting transfers between devices: 32.8 us -> 15.5 us
    all_gather x2 -> x1, waiting for transfers between devices: 0.02 us -> 54.8 us  [local(): expert_in = lax.all_gather(arrived, 'hid', axis=1, tiled=True)]
    unnamed x1 -> x0, other arithmetic: 25 us -> none
    unnamed x34 -> x15, local copies, waits for them, and re-layouts: 20.6 us -> 0.33 us
    all_to_all x7 -> x2, local copies, waits for them, and re-layouts: 20.7 us -> 2.59 us  [local(): lax.all_to_all(out_cols, 'exp', split_axis=0, concat_axis=0, tiled=True)]
    all_to_all x3 -> x2, starting transfers between devices: 32.8 us -> 15.5 us  [the longest x1 11.1 us: local(): lax.all_to_all(out_cols, 'exp', split_axis=0, concat_axis=0, tiled=True)]
    all_to_all x2 -> x1, blocking collectives: 63.9 us -> 48.9 us  [local(): lax.all_to_all(sending, 'exp', split_axis=0, concat_axis=0, tiled=True)]
    all_gather x2 -> x1, blocking collectives: 20.5 us -> 10.4 us  [local(): full_hidden = lax.all_gather(hidden, 'hid', axis=1, tiled=True)]
    all_to_all x3 -> x2, waiting for transfers between devices: 26.7 us -> 21.8 us  [the longest x1 21.8 us: local(): lax.all_to_all(out_cols, 'exp', split_axis=0, concat_axis=0, tiled=True)]
  transfers between devices with their start and end apart: 5 -> 3, of which waited for: 2 -> 2; matrix products, arithmetic and copies ran while one was open for 31% -> 9% of each run, Pallas kernels for 0% -> 0%
where the time goes in v2:
time: 199 us; the launch traced here: 198 us
  waiting for transfers between devices  76.6 us (38%)
  blocking collectives  59.3 us (30%)
  matrix products  16.7 us (8%)
  starting transfers between devices  15.5 us (8%)
  between operations  14.3 us (7%)
  local copies, waits for them, and re-layouts  12.7 us (6%)
  other arithmetic  3.08 us (2%)
    all_gather x1, waiting for transfers between devices, local(): expert_in = lax.all_gather(arrived, 'hid', axis=1, tiled=True)  54.8 us
    all_to_all x1, blocking collectives, local(): lax.all_to_all(sending, 'exp', split_axis=0, concat_axis=0, tiled=True)  48.9 us
    all_to_all x1, waiting for transfers between devices, local(): lax.all_to_all(out_cols, 'exp', split_axis=0, concat_axis=0, tiled=True)  21.8 us
    all_to_all x1, starting transfers between devices, local(): lax.all_to_all(out_cols, 'exp', split_axis=0, concat_axis=0, tiled=True)  11.1 us
    all_gather x1, blocking collectives, local(): full_hidden = lax.all_gather(hidden, 'hid', axis=1, tiled=True)  10.4 us
    dot_general x2, matrix products, rotate(): jnp.einsum('...ab,ca,db->...cd', blocks, paley_table, sylvester_table, pr...  5.15 us
    all_to_all x1, starting transfers between devices, local(): lax.all_to_all(down_parts, 'hid', split_axis=0, concat_axis=0, tiled=True)  4.35 us
  transfers between devices with their start and end apart: 3, of which 2 were waited for; matrix products, arithmetic and copies ran while one was open for 9% of the time, Pallas kernels for 0%

profile of v2, /device:TPU:1, one launch (start us, length us, event | category | flops | bytes accessed | tf_op | source)
XLA Modules:
  0.0 198.2 jit_solution(3465828189842515196)
XLA Ops:
  7.2 0.0 copy-start
  7.2 0.0 all-gather.2.cloned.1.call-start
  7.2 0.9 fusion.46
  8.1 0.1 copy.36
  8.2 0.1 eq.45
  8.3 0.1 fusion.20
  8.4 0.2 reduce_window_sum.17
  8.5 0.2 select_reduce_fusion.1
  8.7 0.1 reshape.42
  8.8 0.1 copy.38
  8.9 0.1 copy.37
  9.0 0.1 eq.49
  9.1 0.1 fusion.19
  9.2 0.2 reduce_window_sum.18
  9.3 0.2 select_reduce_fusion
  9.5 0.1 reshape.43
  9.6 0.1 copy.39
  9.7 0.8 compare_select_fusion
  10.4 0.1 copy.40
  10.5 0.2 fusion.17
  10.8 1.3 convolution_convert_fusion.1
  12.1 1.2 all_to_all.19
  13.3 48.9 %all_to_all.29 = bf16[128,4,1024]{2,1,0:T(4,128)(2,1)S(1)} all-to-all(bf16[128,4,1024]{2,1,0:T(4,128)(2,1)} %all_to_all.19), channel_id=1, replica_groups=mesh['exp'=128,'hid'=4] {'exp'}, dimensions={0} | all-to-all | bytes 2097152 | tf_op jit(solution)/shard_map/all_to_all | solution.py:75
  62.2 1.1 all_to_all.21
  63.3 0.0 all-gather.2.cloned.1.call-update
  63.3 2.9 %reshape_squeeze.3 = bf16[192,4,1024]{2,1,0:T(4,128)(2,1)S(1)} reshape(bf16[1,192,4096]{2,1,0:T(8,128)(2,1)} %param.14) | data formatting | bytes 3145728 | tf_op jit(solution)/shard_map/reshape;squeeze | solution.py:61
  66.2 1.7 copy.41
  67.9 4.3 %all-to-all-start.1 = ((bf16[4,192,1024]{2,1,0:T(8,128)(2,1)}), bf16[4,192,1024]{2,1,0:T(8,128)(2,1)}, u32[]{:S(2)}, u32[]{:S(2)}) async-start(bf16[4,192,1024]{2,1,0:T(8,128)(2,1)} %copy.41), calls=%async_computation.1 | async-start | bytes 3145728 | tf_op jit(solution)/shard_map/all_to_all | solution.py:62
  72.2 54.8 %all-gather.2.cloned.1.call-done = bf16[512,4096]{1,0:T(8,128)(2,1)} async-done(((bf16[512,1024]{1,0:T(8,128)(2,1)}), bf16[512,4096]{1,0:T(8,128)(2,1)}) %all-gather.2.cloned.1.call-update) | async-done | bytes 4194320 | tf_op jit(solution)/shard_map/all_gather | solution.py:76
  127.0 3.9 %fusion.4 = f32[512,192]{0,1:T(8,128)S(1)} fusion(bf16[512,4096]{1,0:T(8,128)(2,1)} %all-gather.2.cloned.1.call-done, bf16[1,192,4096]{2,1,0:T(8,128)(2,1)S(1)} %copy-done), kind=kOutput, calls=%fused_computation.5 | convolution fusion | flops 805306368 | bytes 6160384 | tf_op jit(solution)/shard_map/dot_general | solution.py:77
  130.9 1.5 fusion.12
  132.4 10.4 %all_gather.7 = bf16[512,768]{0,1:T(8,128)(2,1)S(1)} all-gather(bf16[512,192]{0,1:T(8,128)(2,1)S(1)} %fusion.12), channel_id=1, replica_groups=mesh['exp'=128,'hid'=4] {'hid'}, dimensions={1}, use_global_device_ids=true | all-gather | bytes 983040 | tf_op jit(solution)/shard_map/all_gather | solution.py:80
  142.8 2.4 %convolution_convert_fusion = bf16[512,1024]{1,0:T(8,128)(2,1)S(1)} fusion(bf16[512,768]{0,1:T(8,128)(2,1)S(1)} %all_gather.7, bf16[768,1024]{1,0:T(8,128)(2,1)} %bitcast.3), kind=kOutput, calls=%fused_computation.10 | convolution fusion | flops 805830656 | bytes 3407872 | tf_op jit(solution)/shard_map/dot_general | solution.py:81
  145.3 1.3 all_to_all.23
  146.5 11.1 %all-to-all-start.2 = ((bf16[128,4,1024]{2,1,0:T(4,128)(2,1)}), bf16[128,4,1024]{2,1,0:T(4,128)(2,1)}, u32[]{:S(2)}, u32[]{:S(2)}) async-start(bf16[128,4,1024]{2,1,0:T(4,128)(2,1)} %all_to_all.23), calls=%async_computation.2 | async-start | bytes 2097152 | tf_op jit(solution)/shard_map/all_to_all | solution.py:84
  157.7 0.1 copy.42
  157.8 0.1 reshape.49
  157.9 0.1 copy.35
  158.0 0.2 convert_multiply_fusion
  158.2 0.2 copy-done.2
  158.4 2.6 %fusion = f32[12,512,64]{1,0,2:T(8,128)S(1)} fusion(f32[12,12,1]{1,0,2:T(8,128)S(1)} %copy-done.2, f32[512,12,64]{0,2,1:T(8,128)S(1)} %bitcast.33), kind=kOutput, calls=%fused_computation.1 | convolution fusion | flops 56623104 | bytes 3146304 | tf_op jit(solution)/shard_map/...ab,ca,db->...cd/dot_general | solution.py:32
  161.0 2.5 %fusion.6 = f32[12,512,64]{1,2,0:T(8,128)S(1)} fusion(f32[12,512,64]{1,0,2:T(8,128)S(1)} %fusion), kind=kOutput, calls=%fused_computation.7 | convolution fusion | flops 302133248 | bytes 3145728 | tf_op jit(solution)/shard_map/...ab,ca,db->...cd/dot_general | solution.py:32
  163.5 2.4 %fusion.15 = bf16[1,192,768]{2,1,0:T(8,128)(2,1)} fusion(f32[512,768]{0,1:T(8,128)S(1)} %bitcast.34, s32[]{:T(128)S(6)} %select_n.25), kind=kOutput, calls=%fused_computation.16 | convolution fusion | flops 906264576 | bytes 2260996 | tf_op jit(solution)/shard_map/dot_general | solution.py:91
  166.0 21.8 %all-to-all-done.2 = bf16[128,4,1024]{2,1,0:T(4,128)(2,1)} async-done(((bf16[128,4,1024]{2,1,0:T(4,128)(2,1)}), bf16[128,4,1024]{2,1,0:T(4,128)(2,1)}, u32[]{:S(2)}, u32[]{:S(2)}) %all-to-all-start.2) | async-done | bytes 1048608 | tf_op jit(solution)/shard_map/all_to_all | solution.py:84
  187.8 1.3 all_to_all.25
  189.1 1.2 gather_fusion
  190.3 0.4 fusion.16
  190.7 0.6 add_convert_fusion
  (16 shorter events, 0.1 us)
Async XLA Ops:
  7.2 119.8 %copy-start = (bf16[1,192,4096]{2,1,0:T(8,128)(2,1)S(1)}, bf16[1,192,4096]{2,1,0:T(8,128)(2,1)}, u32[]{:S(2)}) copy-start(bf16[1,192,4096]{2,1,0:T(8,128)(2,1)} %param.12) | copy-start | bytes 4718596
  7.2 119.8 %all-gather.2.cloned.1.call-start = ((), (), s32[]{:S(2)}) async-start(), calls=%async_computation.3 | async-start | bytes 5242880 | tf_op jit(solution)/shard_map/all_gather | solution.py:76
  67.9 75.0 %all-to-all-start.1 = ((bf16[4,192,1024]{2,1,0:T(8,128)(2,1)}), bf16[4,192,1024]{2,1,0:T(8,128)(2,1)}, u32[]{:S(2)}, u32[]{:S(2)}) async-start(bf16[4,192,1024]{2,1,0:T(8,128)(2,1)} %copy.41), calls=%async_computation.1 | async-start | bytes 3145728 | tf_op jit(solution)/shard_map/all_to_all | solution.py:62
  72.2 58.6 %copy-start.6 = (bf16[1,192,4096]{2,1,0:T(8,128)(2,1)S(1)}, bf16[1,192,4096]{2,1,0:T(8,128)(2,1)}, u32[]{:S(2)}) copy-start(bf16[1,192,4096]{2,1,0:T(8,128)(2,1)} %param.13) | copy-start | bytes 4718596
  127.0 3.9 %copy-start.5 = (bf16[512,4096]{1,0:T(8,128)(2,1)S(1)}, bf16[512,4096]{1,0:T(8,128)(2,1)}, u32[]{:S(2)}) copy-start(bf16[512,4096]{1,0:T(8,128)(2,1)} %all-gather.2.cloned.1.call-done) | copy-start | bytes 12582916
  146.5 11.3 %copy-start.3 = (f32[32,8]{0,1:T(8,128)S(1)}, f32[32,8]{0,1:T(8,128)}, u32[]{:S(2)}) copy-start(f32[32,8]{0,1:T(8,128)} %param.10) | copy-start | bytes 3076
  146.5 11.4 %copy-start.4 = (s32[1,768]{1,0:T(1,128)S(1)}, s32[1,768]{1,0:T(1,128)}, u32[]{:S(2)}) copy-start(s32[1,768]{1,0:T(1,128)} %param.11) | copy-start | bytes 9220
  146.5 41.2 %all-to-all-start.2 = ((bf16[128,4,1024]{2,1,0:T(4,128)(2,1)}), bf16[128,4,1024]{2,1,0:T(4,128)(2,1)}, u32[]{:S(2)}, u32[]{:S(2)}) async-start(bf16[128,4,1024]{2,1,0:T(4,128)(2,1)} %all_to_all.23), calls=%async_computation.2 | async-start | bytes 2097152 | tf_op jit(solution)/shard_map/all_to_all | solution.py:84
  157.7 0.7 copy-start.2
  189.1 1.6 copy-start.1
Sparse Core Ops, SparseCore 0:
  63.4 63.5 all-gather.1
